TPU v7x, 128 devices: a whole 4x4x4 slice. The times are simulated.
128 devices in a mesh: expert: 32 (over y, z, core), ffn: 4 (over x).
Axes of the slice: x: 4, y: 4, z: 4, core: 2. Of those that a mesh axis runs over, the one named last changes fastest.
Arguments:
- tokens: bfloat16 [16384, 768], P('expert', 'ffn'), may hold values from -6 to 6
- cotangent: bfloat16 [16384, 768], P('expert', 'ffn'), may hold values from -6 to 6
- gates: float32 [16384, 2], P('expert'), may hold values from 0.2 to 1
- expert_ids: int32 [16384, 2], P('expert'), may hold values from 0 to 63, all different within a row; in each aligned block of 512 rows (0 to 511, 512 to 1023, ...) at most 32 rows name the same one
- up_weight: bfloat16 [64, 768, 3072], P('expert', None, 'ffn'), may hold values from -0.21875 to 0.21875
- down_weight: bfloat16 [64, 3072, 768], P('expert', 'ffn'), may hold values from -0.109375 to 0.109375
Outputs:
- layer_out: bfloat16 [16384, 768], P('expert', 'ffn')
- grad_tokens: bfloat16 [16384, 768], P('expert', 'ffn')
- grad_up: bfloat16 [64, 768, 3072], P('expert', None, 'ffn')
- grad_down: bfloat16 [64, 3072, 768], P('expert', 'ffn')
Inputs may be any that keep to these rules, and one draw needn't show every extreme that they name: `expert_ids`: the two experts of a token differ. Among the tokens of one index of expert no expert is named more than 32 times, a bound that some block reaches.
All inputs are finite; a program needn't handle non-finite values.
Results may differ from a plain program's by a relative error of at most 0.0065.
Values may be sent and summed in bfloat16 or wider, within the bound.
No kernel may reach another device: no remote copies, remote signals or barrier semaphores. Data moves between devices by JAX's collectives and lax.ppermute only.
A program may use at most 192 MiB of HBM per device.

v0:
```python
import jax
import jax.numpy as jnp
from jax import lax
from jax.experimental.layout import Layout, with_layout_constraint
from jax.sharding import PartitionSpec as P


def slot_targets(expert_ids, owners, local_experts, capacity):
    flat_ids = expert_ids.reshape(-1)
    count = flat_ids.shape[0]
    experts = owners * local_experts
    columns = lax.broadcasted_iota(jnp.int32, (count, experts), 1)
    onehot = (flat_ids[:, None] == columns).astype(jnp.bfloat16)
    earlier = (
        lax.broadcasted_iota(jnp.int32, (count, count), 0)
        > lax.broadcasted_iota(jnp.int32, (count, count), 1)
    ).astype(jnp.bfloat16)
    before = jnp.dot(earlier, onehot, preferred_element_type=jnp.float32)
    position = jnp.sum(onehot.astype(jnp.float32) * before, axis=1).astype(jnp.int32)
    return (
        flat_ids % local_experts * (owners * capacity)
        + flat_ids // local_experts * capacity
        + position
    )


def shards(tokens, cotangent, gates, expert_ids, up_weight, down_weight):
    owners = lax.axis_size("expert")
    local_experts = up_weight.shape[0]
    experts = owners * local_experts
    tok_rows = tokens.shape[0]
    capacity = 2 * tok_rows // owners
    rows = experts * capacity
    slots = owners * capacity
    target = slot_targets(expert_ids, owners, local_experts, capacity)
    row_ids = lax.broadcasted_iota(jnp.int32, (rows, 2 * tok_rows), 0)
    placer = (row_ids == target[None, :]).astype(jnp.bfloat16)
    tok_ids = lax.broadcasted_iota(jnp.int32, (rows, tok_rows), 0)
    pair = target.reshape(tok_rows, 2)
    token_placer = ((tok_ids == pair[None, :, 0]) | (tok_ids == pair[None, :, 1])).astype(
        jnp.bfloat16
    )
    weights = gates.reshape(-1)
    whole_tokens = lax.all_gather(tokens, "ffn", axis=1, tiled=True)
    whole_cot = lax.all_gather(cotangent, "ffn", axis=1, tiled=True)

    def dispatch(send):
        send = send.astype(jnp.bfloat16).reshape(local_experts, owners, capacity, send.shape[1])
        got = lax.all_to_all(send, "expert", split_axis=1, concat_axis=1, tiled=True)
        return got.reshape(local_experts, slots, got.shape[3])

    rows_in = dispatch(jnp.dot(token_placer, whole_tokens, preferred_element_type=jnp.float32))
    assigned = (weights[:, None] * jnp.repeat(whole_cot, 2, axis=0).astype(jnp.float32)).astype(
        jnp.bfloat16
    )
    grads_in = dispatch(jnp.dot(placer, assigned, preferred_element_type=jnp.float32))

    def send_home(parts):
        cols = jnp.stack(
            [
                lax.psum_scatter(
                    with_layout_constraint(part, Layout((0, 1))),
                    "ffn",
                    scatter_dimension=0,
                    tiled=True,
                )
                for part in parts
            ],
            axis=1,
        ).astype(jnp.bfloat16)
        cols = cols.reshape(cols.shape[0], local_experts, owners, capacity)
        back = lax.all_to_all(cols, "expert", split_axis=2, concat_axis=2, tiled=True)
        return back.reshape(back.shape[0], rows)

    preact = jnp.einsum("xsd,xdf->xsf", rows_in, up_weight, preferred_element_type=jnp.float32)
    gating = jax.nn.sigmoid(preact)
    activated = (preact * gating).astype(jnp.bfloat16)
    out_part = [
        jnp.einsum("fd,sf->ds", down_weight[x], activated[x], preferred_element_type=jnp.float32)
        for x in range(local_experts)
    ]
    out_home = send_home(out_part)
    back_grad = jnp.einsum(
        "xsd,xfd->xsf", grads_in, down_weight, preferred_element_type=jnp.float32
    )
    pre_grad = (back_grad * gating * (1.0 + preact * (1.0 - gating))).astype(jnp.bfloat16)
    grad_down = jnp.einsum(
        "xsf,xsd->xfd", activated, grads_in, preferred_element_type=jnp.float32
    ).astype(jnp.bfloat16)
    grad_up = jnp.einsum(
        "xsd,xsf->xdf", rows_in, pre_grad, preferred_element_type=jnp.float32
    ).astype(jnp.bfloat16)
    in_part = [
        jnp.einsum("df,sf->ds", up_weight[x], pre_grad[x], preferred_element_type=jnp.float32)
        for x in range(local_experts)
    ]
    in_home = send_home(in_part)

    def gather_back(returned):
        picked = lax.dot_general(
            placer, returned, (((0,), (1,)), ((), ())), preferred_element_type=jnp.float32
        )
        return picked.reshape(tok_rows, 2, returned.shape[0])

    layer_out = jnp.sum(gates[:, :, None] * gather_back(out_home), axis=1).astype(jnp.bfloat16)
    grad_tokens = jnp.sum(gather_back(in_home), axis=1).astype(jnp.bfloat16)
    return (layer_out, grad_tokens, grad_up, grad_down)


def solution(mesh):
    placed = (
        P("expert", "ffn"),
        P("expert", "ffn"),
        P("expert", None),
        P("expert", None),
        P("expert", None, "ffn"),
        P("expert", "ffn", None),
    )
    return jax.shard_map(
        shards,
        mesh=mesh,
        in_specs=placed,
        out_specs=(
            P("expert", "ffn"),
            P("expert", "ffn"),
            P("expert", None, "ffn"),
            P("expert", "ffn", None),
        ),
        check_vma=False,
    )
```

profile of v0, /device:TPU:1, one launch (start us, length us, event | category | flops | bytes accessed | tf_op | source)
XLA Modules:
  0.0 334.7 jit_solution(1738526114482320215)
XLA Ops:
  7.2 0.9 copy.55
  8.0 0.7 broadcast_compare_fusion
  8.9 0.6 fusion.35
  10.2 0.3 slice_reduce_fusion.1
  10.5 12.9 %all_gather.6 = bf16[512,768]{0,1:T(8,128)(2,1)S(1)} all-gather(bf16[512,192]{0,1:T(8,128)(2,1)S(1)} %copy-done.3), channel_id=1, replica_groups=mesh['expert'=32,'ffn'=4] {'ffn'}, dimensions={1}, use_global_device_ids=true | all-gather | bytes 983040 | tf_op jit(solution)/shard_map/all_gather | solution.py:44
  23.4 2.1 fusion.6
  25.5 1.9 copy.63
  27.4 10.5 %all-to-all-start = ((bf16[2,32,32,768]{3,2,0,1:T(8,128)(2,1)}), bf16[2,32,32,768]{3,2,0,1:T(8,128)(2,1)S(1)}, u32[]{:S(2)}, u32[]{:S(2)}) async-start(bf16[2,32,32,768]{3,2,0,1:T(8,128)(2,1)} %copy.63), calls=%async_computation | async-start | bytes 6291456 | tf_op jit(solution)/shard_map/all_to_all | solution.py:49
  37.9 13.0 %all_gather.7 = bf16[512,768]{0,1:T(8,128)(2,1)} all-gather(bf16[512,192]{0,1:T(8,128)(2,1)S(1)} %copy-done.4), channel_id=1, replica_groups=mesh['expert'=32,'ffn'=4] {'ffn'}, dimensions={1}, use_global_device_ids=true | all-gather | bytes 983040 | tf_op jit(solution)/shard_map/all_gather | solution.py:45
  50.9 2.5 copy.72
  53.5 4.2 %broadcast_in_dim.2 = f32[512,2,768]{2,1,0:T(2,128)} broadcast(f32[512,768]{1,0:T(8,128)} %copy.72), dimensions={0,2} | broadcast | bytes 4718592 | tf_op jit(solution)/shard_map/broadcast_in_dim | solution.py:53
  57.6 5.4 %convert_element_type.66 = f32[1024,768]{1,0:T(8,128)} reshape(f32[512,2,768]{2,1,0:T(2,128)} %broadcast_in_dim.2) | data formatting | bytes 6291456 | tf_op jit(solution)/shard_map/convert_element_type | solution.py:53
  63.3 6.0 %fusion.9 = bf16[2048,768]{1,0:T(8,128)(2,1)S(1)} fusion(s32[1024]{0:T(1024)S(1)} %fusion.48, f32[1024,768]{1,0:T(8,128)} %convert_element_type.66, f32[1024]{0:T(1024)S(1)} %mul.75), kind=kOutput, calls=%fused_computation.14 | convolution fusion | flops 3226468352 | bytes 6299648 | tf_op jit(solution)/shard_map/dot_general | solution.py:56
  69.4 2.0 copy.73
  71.4 6.3 %all-to-all-done = bf16[2,32,32,768]{3,2,0,1:T(8,128)(2,1)S(1)} async-done(((bf16[2,32,32,768]{3,2,0,1:T(8,128)(2,1)}), bf16[2,32,32,768]{3,2,0,1:T(8,128)(2,1)S(1)}, u32[]{:S(2)}, u32[]{:S(2)}) %all-to-all-start) | async-done | bytes 3145760 | tf_op jit(solution)/shard_map/all_to_all | solution.py:49
  77.7 5.1 %all-to-all-start.2 = ((bf16[2,32,32,768]{3,2,0,1:T(8,128)(2,1)}), bf16[2,32,32,768]{3,2,0,1:T(8,128)(2,1)}, u32[]{:S(2)}, u32[]{:S(2)}) async-start(bf16[2,32,32,768]{3,2,0,1:T(8,128)(2,1)} %copy.73), calls=%async_computation.4 | async-start | bytes 6291456 | tf_op jit(solution)/shard_map/all_to_all | solution.py:49
  83.2 1.7 copy-done.2
  84.9 0.8 copy-done.6
  85.7 5.4 %multiply_convert_fusion.1 = (bf16[2,1024,768]{2,1,0:T(8,128)(2,1)}, f32[2,1024,768]{2,1,0:T(8,128)}) fusion(bf16[2,1024,768]{2,1,0:T(8,128)(2,1)S(1)} %bitcast.59, bf16[2,768,768]{2,1,0:T(8,128)(2,1)S(1)} %copy-done.6), kind=kOutput, calls=%fused_computation.4 | convolution fusion | flops 2423783424 | bytes 14942208 | tf_op jit(solution)/shard_map/xsd,xdf->xsf/dot_general | solution.py:75
  91.1 31.5 %all-to-all-done.2 = bf16[2,32,32,768]{3,2,0,1:T(8,128)(2,1)} async-done(((bf16[2,32,32,768]{3,2,0,1:T(8,128)(2,1)}), bf16[2,32,32,768]{3,2,0,1:T(8,128)(2,1)}, u32[]{:S(2)}, u32[]{:S(2)}) %all-to-all-start.2) | async-done | bytes 3145760 | tf_op jit(solution)/shard_map/all_to_all | solution.py:49
  122.7 2.3 copy.74
  124.9 0.3 copy-done.8
  125.3 6.6 %multiply_convert_fusion = bf16[2,1024,768]{2,1,0:T(8,128)(2,1)S(1)} fusion(f32[2,1024,768]{2,1,0:T(8,128)} %get-tuple-element.7, bf16[2,1024,768]{2,1,0:T(8,128)(2,1)S(1)} %bitcast.57, bf16[2,768,768]{2,1,0:T(8,128)(2,1)S(1)} %copy-done.8), kind=kOutput, calls=%fused_computation.3 | convolution fusion | flops 2430074880 | bytes 14942208 | tf_op jit(solution)/shard_map/xsd,xfd->xsf/dot_general | solution.py:83
  131.9 1.6 copy-done.10
  133.5 3.2 convolution_bitcast_fusion.1
  136.7 4.6 %convolution_bitcast_fusion = f32[768,1024]{1,0:T(8,128)} fusion(bf16[2,1024,768]{2,1,0:T(8,128)(2,1)} %copy-done.10, bf16[2,768,768]{2,1,0:T(8,128)(2,1)S(1)} %copy-done.7), kind=kOutput, calls=%fused_computation.24 | convolution fusion | flops 1207959552 | bytes 5898240 | tf_op jit(solution)/shard_map/df,sf->ds/dot_general | solution.py:94
  141.4 1.6 copy-done.9
  143.0 4.9 %convolution_bitcast_fusion.3 = f32[768,1024]{1,0:T(8,128)} fusion(bf16[2,1024,768]{2,1,0:T(8,128)(2,1)} %get-tuple-element.6, bf16[2,768,768]{2,1,0:T(8,128)(2,1)S(1)} %copy-done.9), kind=kOutput, calls=%fused_computation.27 | convolution fusion | flops 1207959552 | bytes 5898240 | tf_op jit(solution)/shard_map/fd,sf->ds/dot_general | solution.py:79
  148.0 4.5 %convolution_bitcast_fusion.2 = f32[768,1024]{1,0:T(8,128)} fusion(bf16[2,1024,768]{2,1,0:T(8,128)(2,1)} %get-tuple-element.6, bf16[2,768,768]{2,1,0:T(8,128)(2,1)S(1)} %copy-done.9), kind=kOutput, calls=%fused_computation.26 | convolution fusion | flops 1207959552 | bytes 5898240 | tf_op jit(solution)/shard_map/fd,sf->ds/dot_general | solution.py:79
  152.5 1.7 iota_compare_fusion.1
  154.2 7.8 %eq.58 = pred[512,2,2048]{2,1,0:T(4,128)(4,1)} reshape(pred[1024,2048]{1,0:T(8,128)(4,1)S(1)} %iota_compare_fusion.1) | data formatting | bytes 4194304 | tf_op jit(solution)/shard_map/eq | solution.py:37
  162.1 11.0 %reduce-scatter.9.cloned.1.call-done = f32[192,1024]{1,0:T(8,128)} async-done(((f32[768,1024]{1,0:T(8,128)}), f32[192,1024]{1,0:T(8,128)}) %reduce-scatter.9.cloned.1.call-update) | async-done | bytes 786448 | tf_op jit(solution)/shard_map/reduce_scatter | solution.py:61
  173.1 1.2 convert.18
  174.5 39.0 %reduce-scatter.11.cloned.1.call-done = f32[192,1024]{1,0:T(8,128)} async-done(((f32[768,1024]{1,0:T(8,128)}), f32[192,1024]{1,0:T(8,128)}) %reduce-scatter.11.cloned.1.call-update) | async-done | bytes 786448 | tf_op jit(solution)/shard_map/reduce_scatter | solution.py:61
  213.5 1.2 convert.19
  215.1 1.1 copy.77
  216.2 7.8 %all-to-all-start.3 = ((bf16[192,2,32,32]{0,3,1,2:T(8,128)(2,1)}), bf16[192,2,32,32]{0,3,1,2:T(8,128)(2,1)S(1)}, u32[]{:S(2)}, u32[]{:S(2)}) async-start(bf16[192,2,32,32]{0,3,1,2:T(8,128)(2,1)} %copy.77), calls=%async_computation.7 | async-start | bytes 2097152 | tf_op jit(solution)/shard_map/all_to_all | solution.py:72
  224.0 7.5 %convolution_convert_fusion.1 = bf16[2,768,768]{2,1,0:T(8,128)(2,1)} fusion(bf16[2,1024,768]{2,1,0:T(8,128)(2,1)} %bitcast.60, bf16[2,1024,768]{2,1,0:T(8,128)(2,1)} %copy-done.10), kind=kOutput, calls=%fused_computation.23 | convolution fusion | flops 2417098752 | bytes 8650752 | tf_op jit(solution)/shard_map/xsd,xsf->xdf/dot_general | solution.py:90
  231.4 22.5 %reduce-scatter.5.cloned.1.call-done = f32[192,1024]{1,0:T(8,128)} async-done(((f32[768,1024]{1,0:T(8,128)}), f32[192,1024]{1,0:T(8,128)}) %reduce-scatter.5.cloned.1.call-update) | async-done | bytes 786448 | tf_op jit(solution)/shard_map/reduce_scatter | solution.py:61
  254.0 1.2 convert.16
  255.3 38.9 %reduce-scatter.7.cloned.1.call-done = f32[192,1024]{1,0:T(8,128)} async-done(((f32[768,1024]{1,0:T(8,128)}), f32[192,1024]{1,0:T(8,128)}) %reduce-scatter.7.cloned.1.call-update) | async-done | bytes 786448 | tf_op jit(solution)/shard_map/reduce_scatter | solution.py:61
  294.2 1.2 convert.17
  295.9 1.1 copy.67
  297.0 7.8 %all-to-all-start.1 = ((bf16[192,2,32,32]{0,3,1,2:T(8,128)(2,1)}), bf16[192,2,32,32]{0,3,1,2:T(8,128)(2,1)S(1)}, u32[]{:S(2)}, u32[]{:S(2)}) async-start(bf16[192,2,32,32]{0,3,1,2:T(8,128)(2,1)} %copy.67), calls=%async_computation.3 | async-start | bytes 2097152 | tf_op jit(solution)/shard_map/all_to_all | solution.py:72
  304.7 7.1 %convolution_convert_fusion = bf16[2,768,768]{2,1,0:T(8,128)(2,1)} fusion(bf16[2,1024,768]{2,1,0:T(8,128)(2,1)} %get-tuple-element.6, bf16[2,1024,768]{2,1,0:T(8,128)(2,1)} %bitcast.58), kind=kOutput, calls=%fused_computation.22 | convolution fusion | flops 2417098752 | bytes 8650752 | tf_op jit(solution)/shard_map/xsf,xsd->xfd/dot_general | solution.py:87
  311.9 4.3 %fusion.23 = bf16[512,192]{0,1:T(8,128)(2,1)} fusion(bf16[192,2048,1]{0,1,2:T(8,128)(2,1)S(1)} %bitcast.68, pred[512,2,2048]{2,1,0:T(4,128)(4,1)S(1)} %copy-done), kind=kOutput, calls=%fused_computation.35 | convolution fusion | flops 805404672 | bytes 3080192 | tf_op jit(solution)/shard_map/dot_general | solution.py:100
  316.2 5.4 %all-to-all-done.1 = bf16[192,2,32,32]{0,3,1,2:T(8,128)(2,1)S(1)} async-done(((bf16[192,2,32,32]{0,3,1,2:T(8,128)(2,1)}), bf16[192,2,32,32]{0,3,1,2:T(8,128)(2,1)S(1)}, u32[]{:S(2)}, u32[]{:S(2)}) %all-to-all-start.1) | async-done | bytes 786464 | tf_op jit(solution)/shard_map/all_to_all | solution.py:72
  321.7 6.4 %fusion.20 = bf16[512,192]{0,1:T(8,128)(2,1)} fusion(bf16[192,2048,1]{0,1,2:T(8,128)(2,1)S(1)} %bitcast.67, pred[512,2,2048]{2,1,0:T(4,128)(4,1)} %eq.58, f32[512,2]{0,1:T(2,128)S(1)} %copy-done.5), kind=kOutput, calls=%fused_computation.34 | convolution fusion | flops 805601280 | bytes 3084288 | tf_op jit(solution)/shard_map/dot_general | solution.py:100
  (43 shorter events, 3.2 us)
Async XLA Ops:
  7.2 3.4 %copy-start.3 = (bf16[512,192]{0,1:T(8,128)(2,1)S(1)}, bf16[512,192]{0,1:T(8,128)(2,1)}, u32[]{:S(2)}) copy-start(bf16[512,192]{0,1:T(8,128)(2,1)} %param.6) | copy-start | bytes 589828
  27.4 10.5 %copy-start.4 = (bf16[512,192]{0,1:T(8,128)(2,1)S(1)}, bf16[512,192]{0,1:T(8,128)(2,1)}, u32[]{:S(2)}) copy-start(bf16[512,192]{0,1:T(8,128)(2,1)} %param.7) | copy-start | bytes 589828
  27.4 50.2 %all-to-all-start = ((bf16[2,32,32,768]{3,2,0,1:T(8,128)(2,1)}), bf16[2,32,32,768]{3,2,0,1:T(8,128)(2,1)S(1)}, u32[]{:S(2)}, u32[]{:S(2)}) async-start(bf16[2,32,32,768]{3,2,0,1:T(8,128)(2,1)} %copy.63), calls=%async_computation | async-start | bytes 6291456 | tf_op jit(solution)/shard_map/all_to_all | solution.py:49
  57.6 5.4 %copy-start.5 = (f32[512,2]{0,1:T(2,128)S(1)}, f32[512,2]{0,1:T(2,128)}, u32[]{:S(2)}) copy-start(f32[512,2]{0,1:T(2,128)} %param.8) | copy-start | bytes 12292
  77.7 45.0 %all-to-all-start.2 = ((bf16[2,32,32,768]{3,2,0,1:T(8,128)(2,1)}), bf16[2,32,32,768]{3,2,0,1:T(8,128)(2,1)}, u32[]{:S(2)}, u32[]{:S(2)}) async-start(bf16[2,32,32,768]{3,2,0,1:T(8,128)(2,1)} %copy.73), calls=%async_computation.4 | async-start | bytes 6291456 | tf_op jit(solution)/shard_map/all_to_all | solution.py:49
  82.7 90.3 %reduce-scatter.9.cloned.1.call-start = ((), (), s32[]{:S(2)}) async-start(), calls=%async_computation.10 | async-start | bytes 3932160 | tf_op jit(solution)/shard_map/reduce_scatter | solution.py:61
  83.0 2.8 copy-start.6
  83.2 1.7 copy-start.2
  122.6 2.6 copy-start.8
  124.9 6.9 %copy-start.1 = (bf16[2,32,32,768]{3,2,1,0:T(8,128)(2,1)}, bf16[2,32,32,768]{3,2,1,0:T(8,128)(2,1)S(1)}, u32[]{:S(2)}) copy-start(bf16[2,32,32,768]{3,2,1,0:T(8,128)(2,1)S(1)} %copy.74) | copy-start | bytes 9437188
  125.3 8.2 %copy-start.7 = (bf16[2,768,768]{2,1,0:T(8,128)(2,1)S(1)}, bf16[2,768,768]{2,1,0:T(8,128)(2,1)}, u32[]{:S(2)}) copy-start(bf16[2,768,768]{2,1,0:T(8,128)(2,1)} %param.10) | copy-start | bytes 7077892
  131.8 1.6 copy-start.10
  136.7 76.8 %reduce-scatter.11.cloned.1.call-start = ((), (), s32[]{:S(2)}) async-start(), calls=%async_computation.11 | async-start | bytes 3932160 | tf_op jit(solution)/shard_map/reduce_scatter | solution.py:61
  141.3 1.7 copy-start.9
  141.3 112.6 %reduce-scatter.5.cloned.1.call-start = ((), (), s32[]{:S(2)}) async-start(), calls=%async_computation.8 | async-start | bytes 3932160 | tf_op jit(solution)/shard_map/reduce_scatter | solution.py:61
  147.9 146.3 %reduce-scatter.7.cloned.1.call-start = ((), (), s32[]{:S(2)}) async-start(), calls=%async_computation.9 | async-start | bytes 3932160 | tf_op jit(solution)/shard_map/reduce_scatter | solution.py:61
  216.2 80.8 %all-to-all-start.3 = ((bf16[192,2,32,32]{0,3,1,2:T(8,128)(2,1)}), bf16[192,2,32,32]{0,3,1,2:T(8,128)(2,1)S(1)}, u32[]{:S(2)}, u32[]{:S(2)}) async-start(bf16[192,2,32,32]{0,3,1,2:T(8,128)(2,1)} %copy.77), calls=%async_computation.7 | async-start | bytes 2097152 | tf_op jit(solution)/shard_map/all_to_all | solution.py:72
  297.0 24.7 %all-to-all-start.1 = ((bf16[192,2,32,32]{0,3,1,2:T(8,128)(2,1)}), bf16[192,2,32,32]{0,3,1,2:T(8,128)(2,1)S(1)}, u32[]{:S(2)}, u32[]{:S(2)}) async-start(bf16[192,2,32,32]{0,3,1,2:T(8,128)(2,1)} %copy.67), calls=%async_computation.3 | async-start | bytes 2097152 | tf_op jit(solution)/shard_map/all_to_all | solution.py:72
  304.7 7.2 %copy-start = (pred[512,2,2048]{2,1,0:T(4,128)(4,1)S(1)}, pred[512,2,2048]{2,1,0:T(4,128)(4,1)}, u32[]{:S(2)}) copy-start(pred[512,2,2048]{2,1,0:T(4,128)(4,1)} %eq.58) | copy-start | bytes 6291460
Sparse Core Ops, SparseCore 0:
  136.8 36.2 reduce-scatter.8
  175.5 37.9 reduce-scatter.10
  215.9 37.9 reduce-scatter.4
  256.2 37.9 reduce-scatter.6
where the time goes:
time: 336 us; the launch traced here: 335 us
  waiting for transfers between devices  155 us (46%)
  matrix products  63.1 us (19%)
  local copies, waits for them, and re-layouts  37.5 us (11%)
  starting transfers between devices  31.5 us (9%)
  blocking collectives  25.9 us (8%)
  between operations  14.1 us (4%)
  other arithmetic  7.85 us (2%)
    reduce_scatter x4, waiting for transfers between devices, send_home(): lax.psum_scatter(with_layout_constraint(part, Layout((0, 1))), 'ffn', sca...  111 us
    all_to_all x2, waiting for transfers between devices, dispatch(): lax.all_to_all(send, 'expert', split_axis=1, concat_axis=1, tiled=True)  37.8 us
    all_to_all x2, starting transfers between devices, dispatch(): lax.all_to_all(send, 'expert', split_axis=1, concat_axis=1, tiled=True)  15.6 us
    all_to_all x2, starting transfers between devices, send_home(): lax.all_to_all(cols, 'expert', split_axis=2, concat_axis=2, tiled=True)  15.6 us
    all_gather x1, blocking collectives, shards(): whole_cot = lax.all_gather(cotangent, 'ffn', axis=1, tiled=True)  13 us
    all_gather x1, blocking collectives, shards(): whole_tokens = lax.all_gather(tokens, 'ffn', axis=1, tiled=True)  12.9 us
    dot_general x2, matrix products, gather_back(): lax.dot_general(placer, returned, (((0,), (1,)), ((), ())), preferred_ele...  10.7 us
    dot_general x2, matrix products, shards(): jnp.einsum('fd,sf->ds', down_weight[x], activated[x], preferred_element_t...  9.43 us
  transfers between devices with their start and end apart: 8, of which 7 were waited for; matrix products, arithmetic and copies ran while one was open for 23% of the time, Pallas kernels for 0%

commit v1 on v0

--- a/solution.py
+++ b/solution.py
@@ -42,7 +42,13 @@
     )
     weights = gates.reshape(-1)
     whole_tokens = lax.all_gather(tokens, "ffn", axis=1, tiled=True)
-    whole_cot = lax.all_gather(cotangent, "ffn", axis=1, tiled=True)
+    degree = lax.axis_size("ffn")
+    samples = []
+    for to_i in range(cotangent.ndim):
+        samples.append(degree if to_i == 1 else 1)
+    whole_cot = lax.all_to_all(
+        jnp.tile(cotangent, samples), "ffn", split_axis=1, concat_axis=1, tiled=True
+    )
 
     def dispatch(send):
         send = send.astype(jnp.bfloat16).reshape(local_experts, owners, capacity, send.shape[1])

time: 336 us -> 300 us (0.89)
  waiting for transfers between devices: 155 us -> 63.6 us
  blocking collectives: 25.9 us -> 106 us
  starting transfers between devices: 31.5 us -> 16.1 us
  local copies, waits for them, and re-layouts: 37.5 us -> 32.1 us
  matrix products: 63.1 us -> 58.5 us
    all_to_all x0 -> x2, blocking collectives: none -> 93.4 us  [dispatch(): lax.all_to_all(send, 'expert', split_axis=1, concat_axis=1, tiled=True)]
    reduce_scatter x4, waiting for transfers between devices: 111 us -> 43.6 us  [send_home(): lax.psum_scatter(with_layout_constraint(part, Layout((0, 1))), 'ffn', sca...]
    all_to_all x2 -> x1, waiting for transfers between devices: 37.8 us -> 14.6 us  [shards(): lax.all_to_all(jnp.tile(cotangent, samples), 'ffn', split_axis=1, concat_...]
    all_gather x1 -> x0, blocking collectives: 13 us -> none  [shards(): whole_cot = lax.all_gather(cotangent, 'ffn', axis=1, tiled=True)]
    all_to_all x2 -> x1, starting transfers between devices: 15.6 us -> 4.13 us  [shards(): lax.all_to_all(jnp.tile(cotangent, samples), 'ffn', split_axis=1, concat_...]
    all_to_all x2, starting transfers between devices: 15.6 us -> 11.7 us  [send_home(): lax.all_to_all(cols, 'expert', split_axis=2, concat_axis=2, tiled=True)]
    unnamed x24 -> x30, local copies, waits for them, and re-layouts: 7.06 us -> 10.7 us
  transfers between devices with their start and end apart: 8 -> 7, of which waited for: 7 -> 4; matrix products, arithmetic and copies ran while one was open for 23% -> 23% of each run, Pallas kernels for 0% -> 0%
where the time goes in v1:
time: 300 us; the launch traced here: 299 us
  blocking collectives  106 us (35%)
  waiting for transfers between devices  63.6 us (21%)
  matrix products  58.5 us (20%)
  local copies, waits for them, and re-layouts  32.1 us (11%)
  starting transfers between devices  16.1 us (5%)
  between operations  14.1 us (5%)
  other arithmetic  8.13 us (3%)
    all_to_all x2, blocking collectives, dispatch(): lax.all_to_all(send, 'expert', split_axis=1, concat_axis=1, tiled=True)  93.4 us
    reduce_scatter x4, waiting for transfers between devices, send_home(): lax.psum_scatter(with_layout_constraint(part, Layout((0, 1))), 'ffn', sca...  43.6 us
    all_to_all x1, waiting for transfers between devices, shards(): lax.all_to_all(jnp.tile(cotangent, samples), 'ffn', split_axis=1, concat_...  14.6 us
    all_gather x1, blocking collectives, shards(): whole_tokens = lax.all_gather(tokens, 'ffn', axis=1, tiled=True)  12.9 us
    all_to_all x2, starting transfers between devices, send_home(): lax.all_to_all(cols, 'expert', split_axis=2, concat_axis=2, tiled=True)  11.7 us
    dot_general x2, matrix products, gather_back(): lax.dot_general(placer, returned, (((0,), (1,)), ((), ())), preferred_ele...  10.7 us
    unnamed x30, local copies, waits for them, and re-layouts  10.7 us
    dot_general x2, matrix products, shards(): jnp.einsum('fd,sf->ds', down_weight[x], activated[x], preferred_element_t...  8.38 us
  transfers between devices with their start and end apart: 7, of which 4 were waited for; matrix products, arithmetic and copies ran while one was open for 23% of the time, Pallas kernels for 0%

profile of v1, /device:TPU:1, one launch (start us, length us, event | category | flops | bytes accessed | tf_op | source)
XLA Modules:
  0.0 298.9 jit_solution(17932421227807978051)
XLA Ops:
  7.2 0.9 copy.55
  8.1 0.7 broadcast_compare_fusion
  9.0 0.6 fusion.35
  10.0 0.3 fusion.38
  10.3 0.3 slice_reduce_fusion.1
  10.6 12.9 %all_gather.3 = bf16[512,768]{0,1:T(8,128)(2,1)S(1)} all-gather(bf16[512,192]{0,1:T(8,128)(2,1)S(1)} %copy-done.3), channel_id=1, replica_groups=mesh['expert'=32,'ffn'=4] {'ffn'}, dimensions={1}, use_global_device_ids=true | all-gather | bytes 983040 | tf_op jit(solution)/shard_map/all_gather | solution.py:44
  23.5 2.1 fusion.6
  25.5 0.3 copy.63
  25.8 49.5 %all_to_all.26 = bf16[2,32,32,768]{3,2,0,1:T(8,128)(2,1)S(1)} all-to-all(bf16[2,32,32,768]{3,2,0,1:T(8,128)(2,1)S(1)} %copy.63), channel_id=1, replica_groups=mesh['expert'=32,'ffn'=4] {'expert'}, dimensions={1} | all-to-all | bytes 6291456 | tf_op jit(solution)/shard_map/all_to_all | solution.py:55
  75.6 2.5 copy-done.8
  78.1 5.1 %multiply_convert_fusion.1 = (bf16[2,1024,768]{2,1,0:T(8,128)(2,1)S(1)}, f32[2,1024,768]{2,1,0:T(8,128)}) fusion(bf16[2,1024,768]{2,1,0:T(8,128)(2,1)S(1)} %bitcast.60, bf16[2,768,768]{2,1,0:T(8,128)(2,1)S(1)} %copy-done.8), kind=kOutput, calls=%fused_computation.4 | convolution fusion | flops 2423783424 | bytes 14942208 | tf_op jit(solution)/shard_map/xsd,xdf->xsf/dot_general | solution.py:81
  83.2 1.6 copy-done.11
  84.9 3.1 %convolution_bitcast_fusion.3 = f32[768,1024]{1,0:T(8,128)} fusion(bf16[2,1024,768]{2,1,0:T(8,128)(2,1)S(1)} %get-tuple-element.6, bf16[2,768,768]{2,1,0:T(8,128)(2,1)S(1)} %copy-done.6), kind=kOutput, calls=%fused_computation.27 | convolution fusion | flops 1207959552 | bytes 5898240 | tf_op jit(solution)/shard_map/fd,sf->ds/dot_general | solution.py:85
  88.0 0.9 copy-done.4
  88.9 0.9 tile.2
  89.8 4.1 %all-to-all-start.2 = ((bf16[512,4,192]{0,2,1:T(8,128)(2,1)}), bf16[512,4,192]{0,2,1:T(8,128)(2,1)S(1)}, u32[]{:S(2)}, u32[]{:S(2)}) async-start(bf16[512,4,192]{0,2,1:T(8,128)(2,1)} %tile.2), calls=%async_computation.4 | async-start | bytes 1572864 | tf_op jit(solution)/shard_map/all_to_all | solution.py:49
  93.9 5.3 %convolution_bitcast_fusion.2 = f32[768,1024]{1,0:T(8,128)} fusion(bf16[2,1024,768]{2,1,0:T(8,128)(2,1)} %copy-done.11, bf16[2,768,768]{2,1,0:T(8,128)(2,1)} %param.11), kind=kOutput, calls=%fused_computation.26 | convolution fusion | flops 1207959552 | bytes 5898240 | tf_op jit(solution)/shard_map/fd,sf->ds/dot_general | solution.py:85
  99.5 0.4 copy-done.5
  100.3 14.6 %all-to-all-done.2 = bf16[512,4,192]{0,2,1:T(8,128)(2,1)S(1)} async-done(((bf16[512,4,192]{0,2,1:T(8,128)(2,1)}), bf16[512,4,192]{0,2,1:T(8,128)(2,1)S(1)}, u32[]{:S(2)}, u32[]{:S(2)}) %all-to-all-start.2) | async-done | bytes 786464 | tf_op jit(solution)/shard_map/all_to_all | solution.py:49
  114.8 0.3 bitcast_convert_fusion
  115.1 1.6 copy.72
  116.7 2.5 broadcast_in_dim.2
  119.2 3.4 %convert_element_type.70 = f32[1024,768]{1,0:T(8,128)} reshape(f32[512,2,768]{2,1,0:T(2,128)S(1)} %broadcast_in_dim.2) | data formatting | bytes 6291456 | tf_op jit(solution)/shard_map/convert_element_type | solution.py:59
  122.6 6.0 %fusion.9 = bf16[2048,768]{1,0:T(8,128)(2,1)S(1)} fusion(s32[1024]{0:T(1024)S(1)} %fusion.48, f32[1024,768]{1,0:T(8,128)} %convert_element_type.70, f32[1024]{0:T(1024)S(1)} %mul.75), kind=kOutput, calls=%fused_computation.14 | convolution fusion | flops 3226468352 | bytes 6299648 | tf_op jit(solution)/shard_map/dot_general | solution.py:62
  128.7 0.3 copy.73
  129.0 43.8 %all_to_all.27 = bf16[2,32,32,768]{3,2,0,1:T(8,128)(2,1)S(1)} all-to-all(bf16[2,32,32,768]{3,2,0,1:T(8,128)(2,1)S(1)} %copy.73), channel_id=1, replica_groups=mesh['expert'=32,'ffn'=4] {'expert'}, dimensions={1} | all-to-all | bytes 6291456 | tf_op jit(solution)/shard_map/all_to_all | solution.py:55
  173.1 2.5 copy-done.7
  175.6 3.8 %multiply_convert_fusion = bf16[2,1024,768]{2,1,0:T(8,128)(2,1)S(1)} fusion(f32[2,1024,768]{2,1,0:T(8,128)S(1)} %bitcast.73, bf16[2,1024,768]{2,1,0:T(8,128)(2,1)S(1)} %bitcast.62, bf16[2,768,768]{2,1,0:T(8,128)(2,1)S(1)} %copy-done.7), kind=kOutput, calls=%fused_computation.3 | convolution fusion | flops 2430074880 | bytes 14942208 | tf_op jit(solution)/shard_map/xsd,xfd->xsf/dot_general | solution.py:89
  179.4 1.6 copy-done.10
  181.0 3.2 %convolution_bitcast_fusion.1 = f32[768,1024]{1,0:T(8,128)} fusion(bf16[2,1024,768]{2,1,0:T(8,128)(2,1)S(1)} %multiply_convert_fusion, bf16[2,768,768]{2,1,0:T(8,128)(2,1)S(1)} %copy-done.9), kind=kOutput, calls=%fused_computation.25 | convolution fusion | flops 1207959552 | bytes 5898240 | tf_op jit(solution)/shard_map/df,sf->ds/dot_general | solution.py:100
  184.3 4.6 %convolution_bitcast_fusion = f32[768,1024]{1,0:T(8,128)} fusion(bf16[2,1024,768]{2,1,0:T(8,128)(2,1)} %copy-done.10, bf16[2,768,768]{2,1,0:T(8,128)(2,1)S(1)} %copy-done.9), kind=kOutput, calls=%fused_computation.24 | convolution fusion | flops 1207959552 | bytes 5898240 | tf_op jit(solution)/shard_map/df,sf->ds/dot_general | solution.py:100
  188.9 1.7 iota_compare_fusion.1
  190.6 7.8 %eq.58 = pred[512,2,2048]{2,1,0:T(4,128)(4,1)} reshape(pred[1024,2048]{1,0:T(8,128)(4,1)S(1)} %iota_compare_fusion.1) | data formatting | bytes 4194304 | tf_op jit(solution)/shard_map/eq | solution.py:37
  198.4 1.2 convert.17
  199.8 1.2 convert.18
  201.5 1.1 copy.67
  202.5 4.0 %all-to-all-start.1 = ((bf16[192,2,32,32]{0,3,1,2:T(8,128)(2,1)}), bf16[192,2,32,32]{0,3,1,2:T(8,128)(2,1)S(1)}, u32[]{:S(2)}, u32[]{:S(2)}) async-start(bf16[192,2,32,32]{0,3,1,2:T(8,128)(2,1)} %copy.67), calls=%async_computation.3 | async-start | bytes 2097152 | tf_op jit(solution)/shard_map/all_to_all | solution.py:78
  206.5 7.0 %convolution_convert_fusion.1 = bf16[2,768,768]{2,1,0:T(8,128)(2,1)} fusion(bf16[2,1024,768]{2,1,0:T(8,128)(2,1)} %bitcast.61, bf16[2,1024,768]{2,1,0:T(8,128)(2,1)} %copy-done.10), kind=kOutput, calls=%fused_computation.23 | convolution fusion | flops 2417098752 | bytes 8650752 | tf_op jit(solution)/shard_map/xsd,xsf->xdf/dot_general | solution.py:96
  213.5 4.7 %reduce-scatter.9.cloned.1.call-done = f32[192,1024]{1,0:T(8,128)} async-done(((f32[768,1024]{1,0:T(8,128)}), f32[192,1024]{1,0:T(8,128)}) %reduce-scatter.9.cloned.1.call-update) | async-done | bytes 786448 | tf_op jit(solution)/shard_map/reduce_scatter | solution.py:67
  218.2 1.2 convert.19
  219.6 38.9 %reduce-scatter.11.cloned.1.call-done = f32[192,1024]{1,0:T(8,128)} async-done(((f32[768,1024]{1,0:T(8,128)}), f32[192,1024]{1,0:T(8,128)}) %reduce-scatter.11.cloned.1.call-update) | async-done | bytes 786448 | tf_op jit(solution)/shard_map/reduce_scatter | solution.py:67
  258.5 1.2 convert.20
  260.1 1.1 copy.77
  261.2 7.8 %all-to-all-start.4 = ((bf16[192,2,32,32]{0,3,1,2:T(8,128)(2,1)}), bf16[192,2,32,32]{0,3,1,2:T(8,128)(2,1)S(1)}, u32[]{:S(2)}, u32[]{:S(2)}) async-start(bf16[192,2,32,32]{0,3,1,2:T(8,128)(2,1)} %copy.77), calls=%async_computation.8 | async-start | bytes 2097152 | tf_op jit(solution)/shard_map/all_to_all | solution.py:78
  269.0 7.1 %convolution_convert_fusion = bf16[2,768,768]{2,1,0:T(8,128)(2,1)} fusion(bf16[2,1024,768]{2,1,0:T(8,128)(2,1)} %copy-done.11, bf16[2,1024,768]{2,1,0:T(8,128)(2,1)} %bitcast.63), kind=kOutput, calls=%fused_computation.22 | convolution fusion | flops 2417098752 | bytes 8650752 | tf_op jit(solution)/shard_map/xsf,xsd->xfd/dot_general | solution.py:93
  276.2 4.3 %fusion.20 = bf16[512,192]{0,1:T(8,128)(2,1)} fusion(bf16[192,2048,1]{0,1,2:T(8,128)(2,1)S(1)} %bitcast.71, pred[512,2,2048]{2,1,0:T(4,128)(4,1)S(1)} %copy-done, f32[512,2]{0,1:T(2,128)S(1)} %copy-done.5), kind=kOutput, calls=%fused_computation.34 | convolution fusion | flops 805601280 | bytes 3084288 | tf_op jit(solution)/shard_map/dot_general | solution.py:106
  280.4 5.4 %all-to-all-done.4 = bf16[192,2,32,32]{0,3,1,2:T(8,128)(2,1)S(1)} async-done(((bf16[192,2,32,32]{0,3,1,2:T(8,128)(2,1)}), bf16[192,2,32,32]{0,3,1,2:T(8,128)(2,1)S(1)}, u32[]{:S(2)}, u32[]{:S(2)}) %all-to-all-start.4) | async-done | bytes 786464 | tf_op jit(solution)/shard_map/all_to_all | solution.py:78
  285.9 6.4 %fusion.23 = bf16[512,192]{0,1:T(8,128)(2,1)} fusion(bf16[192,2048,1]{0,1,2:T(8,128)(2,1)S(1)} %bitcast.70, pred[512,2,2048]{2,1,0:T(4,128)(4,1)} %eq.58), kind=kOutput, calls=%fused_computation.35 | convolution fusion | flops 805404672 | bytes 3080192 | tf_op jit(solution)/shard_map/dot_general | solution.py:106
  (51 shorter events, 3.2 us)
Async XLA Ops:
  7.2 3.4 %copy-start.3 = (bf16[512,192]{0,1:T(8,128)(2,1)S(1)}, bf16[512,192]{0,1:T(8,128)(2,1)}, u32[]{:S(2)}) copy-start(bf16[512,192]{0,1:T(8,128)(2,1)} %param.6) | copy-start | bytes 589828
  7.2 191.2 %reduce-scatter.5.cloned.1.call-start = ((), (), s32[]{:S(2)}) async-start(), calls=%async_computation.9 | async-start | bytes 3932160 | tf_op jit(solution)/shard_map/reduce_scatter | solution.py:67
  75.4 2.8 copy-start.8
  75.6 7.6 %copy-start.1 = (bf16[2,32,32,768]{3,2,1,0:T(8,128)(2,1)}, bf16[2,32,32,768]{3,2,1,0:T(8,128)(2,1)S(1)}, u32[]{:S(2)}) copy-start(bf16[2,32,32,768]{3,2,1,0:T(8,128)(2,1)S(1)} %copy.64) | copy-start | bytes 9437188
  78.1 6.7 %copy-start.6 = (bf16[2,768,768]{2,1,0:T(8,128)(2,1)S(1)}, bf16[2,768,768]{2,1,0:T(8,128)(2,1)}, u32[]{:S(2)}) copy-start(bf16[2,768,768]{2,1,0:T(8,128)(2,1)} %param.11) | copy-start | bytes 7077892
  83.2 1.6 copy-start.11
  87.9 0.9 copy-start.4
  89.8 25.0 %all-to-all-start.2 = ((bf16[512,4,192]{0,2,1:T(8,128)(2,1)}), bf16[512,4,192]{0,2,1:T(8,128)(2,1)S(1)}, u32[]{:S(2)}, u32[]{:S(2)}) async-start(bf16[512,4,192]{0,2,1:T(8,128)(2,1)} %tile.2), calls=%async_computation.4 | async-start | bytes 1572864 | tf_op jit(solution)/shard_map/all_to_all | solution.py:49
  93.9 105.9 %reduce-scatter.7.cloned.1.call-start = ((), (), s32[]{:S(2)}) async-start(), calls=%async_computation.10 | async-start | bytes 3932160 | tf_op jit(solution)/shard_map/reduce_scatter | solution.py:67
  99.2 0.7 copy-start.5
  99.3 118.9 %reduce-scatter.9.cloned.1.call-start = ((), (), s32[]{:S(2)}) async-start(), calls=%async_computation.11 | async-start | bytes 3932160 | tf_op jit(solution)/shard_map/reduce_scatter | solution.py:67
  128.7 44.4 %slice-start = ((s8[6291456]{0:T(1024)(128)(4,1)}), s8[4194304]{0:T(1024)(128)(4,1)S(1)}, s32[]{:S(2)}) async-start(s8[6291456]{0:T(1024)(128)(4,1)} %bitcast.72), calls=%async_computation.13 | async-start | bytes 8388608
  129.0 44.1 %slice-start.1 = ((s8[6291456]{0:T(1024)(128)(4,1)}), s8[2097152]{0:T(1024)(128)(4,1)S(1)}, s32[]{:S(2)}) async-start(s8[6291456]{0:T(1024)(128)(4,1)} %bitcast.72), calls=%async_computation.14 | async-start | bytes 4194304
  172.8 2.8 copy-start.7
  173.0 6.4 %copy-start.2 = (bf16[2,32,32,768]{3,2,1,0:T(8,128)(2,1)}, bf16[2,32,32,768]{3,2,1,0:T(8,128)(2,1)S(1)}, u32[]{:S(2)}) copy-start(bf16[2,32,32,768]{3,2,1,0:T(8,128)(2,1)S(1)} %copy.74) | copy-start | bytes 9437188
  175.6 5.5 %copy-start.9 = (bf16[2,768,768]{2,1,0:T(8,128)(2,1)S(1)}, bf16[2,768,768]{2,1,0:T(8,128)(2,1)}, u32[]{:S(2)}) copy-start(bf16[2,768,768]{2,1,0:T(8,128)(2,1)} %param.10) | copy-start | bytes 7077892
  179.4 1.6 copy-start.10
  184.2 74.3 %reduce-scatter.11.cloned.1.call-start = ((), (), s32[]{:S(2)}) async-start(), calls=%async_computation.12 | async-start | bytes 3932160 | tf_op jit(solution)/shard_map/reduce_scatter | solution.py:67
  202.5 58.7 %all-to-all-start.1 = ((bf16[192,2,32,32]{0,3,1,2:T(8,128)(2,1)}), bf16[192,2,32,32]{0,3,1,2:T(8,128)(2,1)S(1)}, u32[]{:S(2)}, u32[]{:S(2)}) async-start(bf16[192,2,32,32]{0,3,1,2:T(8,128)(2,1)} %copy.67), calls=%async_computation.3 | async-start | bytes 2097152 | tf_op jit(solution)/shard_map/all_to_all | solution.py:78
  261.2 24.7 %all-to-all-start.4 = ((bf16[192,2,32,32]{0,3,1,2:T(8,128)(2,1)}), bf16[192,2,32,32]{0,3,1,2:T(8,128)(2,1)S(1)}, u32[]{:S(2)}, u32[]{:S(2)}) async-start(bf16[192,2,32,32]{0,3,1,2:T(8,128)(2,1)} %copy.77), calls=%async_computation.8 | async-start | bytes 2097152 | tf_op jit(solution)/shard_map/all_to_all | solution.py:78
  269.0 7.2 %copy-start = (pred[512,2,2048]{2,1,0:T(4,128)(4,1)S(1)}, pred[512,2,2048]{2,1,0:T(4,128)(4,1)}, u32[]{:S(2)}) copy-start(pred[512,2,2048]{2,1,0:T(4,128)(4,1)} %eq.58) | copy-start | bytes 6291460
Sparse Core Ops, SparseCore 0:
  88.1 44.3 reduce-scatter.4
  134.9 34.7 reduce-scatter.6
  184.3 33.8 reduce-scatter.8
  220.5 37.9 reduce-scatter.10
